TPU v7x, 32 devices: a whole 2x2x4 slice. The times are simulated.
32 devices in a mesh: ctx: 4 (over y, core), row: 8 (over z, x).
Axes of the slice: x: 2, y: 2, z: 4, core: 2. Of those that a mesh axis runs over, the one named last changes fastest.
Arguments:
- queries: bfloat16 [16, 2, 4096], P('row'), may hold values from -400 to 400
- prefix_id: int32 [16], P('row'), may hold values from 0 to 7
- prefix_keys: bfloat16 [8, 1024, 512], P(None, ('ctx', 'row')), may hold values from -8 to 8
- prefix_values: bfloat16 [8, 1024, 512], P(None, ('ctx', 'row')), may hold values from -6 to 6
- pool_keys: bfloat16 [512, 64, 512], P(('ctx', 'row')), may hold values from -5 to 5
- pool_values: bfloat16 [512, 64, 512], P(('ctx', 'row')), may hold values from -6 to 6
- page_table: int32 [16, 32], P('row'), may hold values from 0 to 511, as said below
- suffix_len: int32 [16], P('row'), may hold values from 256 to 2048
- new_keys: bfloat16 [16, 2, 512], P('row'), may hold values from -6.25 to 6.25
- new_values: bfloat16 [16, 2, 512], P('row'), may hold values from -6 to 6
Outputs:
- attended: bfloat16 [16, 2, 4096], P('row')
Inputs may be any that keep to these rules, and one draw needn't show every extreme that they name: `page_table`: the 64 entries of the rows i with one value of i // 2 name different pool pages p with (p // 16) % (8) == i // 2, and together they name all such pages.
All inputs are finite; a program needn't handle non-finite values.
Results may differ from a plain program's by a relative error of at most 0.003.
Values may be sent and summed in bfloat16 or wider, within the bound.
No kernel may reach another device: no remote copies, remote signals or barrier semaphores. Data moves between devices by JAX's collectives and lax.ppermute only.
A program may use at most 64 MiB of HBM per device.

v0:
```python
import math
import jax
import jax.numpy as jnp
from jax import lax
from jax.sharding import PartitionSpec as P

H = 32
KVH = 4
HD = 128
MASKED_SCORE = -1e30


def joined(value, axis, join):
    pieces = jax.tree.map(lambda part: lax.all_gather(part, axis), value)
    head = jax.tree.map(lambda part: part[0], pieces)
    tail = jax.tree.map(lambda part: part[1:], pieces)
    running, _ = lax.scan(lambda running, share: (join(running, share), None), head, tail)
    return running


def combine_pair(earlier, later):
    highest = jnp.maximum(earlier[0], later[0])
    left_factor = jnp.exp(earlier[0] - highest)
    right_factor = jnp.exp(later[0] - highest)
    totals = left_factor * earlier[1] + right_factor * later[1]
    sums = left_factor[..., None] * earlier[2] + right_factor[..., None] * later[2]
    return (highest, totals, sums)


def fold_stack(stacked):
    peak_stack, total_stack, sum_stack = stacked
    highest = jnp.max(peak_stack, axis=0)
    factor = jnp.exp(peak_stack - highest[None])
    return (
        highest,
        jnp.sum(factor * total_stack, axis=0),
        jnp.sum(factor[..., None] * sum_stack, axis=0),
    )


def block_stats(scores, valid_mask, values, einsum_form):
    block_peak = jnp.max(jnp.where(valid_mask, scores, MASKED_SCORE), axis=-1)
    weights = jnp.where(valid_mask, jnp.exp(scores - block_peak[..., None]), 0.0).astype(
        jnp.bfloat16
    )
    block_total = jnp.sum(weights.astype(jnp.float32), axis=-1)
    block_sum = jnp.einsum(einsum_form, weights, values, preferred_element_type=jnp.float32)
    return (block_peak, block_total, block_sum)


def heads_merged(stats):
    lead = stats[0].shape[:2]
    return (
        stats[0].reshape(lead + (H,)),
        stats[1].reshape(lead + (H,)),
        stats[2].reshape(lead + (H, HD)),
    )


def per_device(
    queries,
    prefix_id,
    prefix_keys,
    prefix_values,
    pool_keys,
    pool_values,
    page_table,
    suffix_len,
    new_keys,
    new_values,
):
    rows_dev, step_count, feature_width = queries.shape
    groups = H // KVH
    score_scale = 1.0 / math.sqrt(HD)
    row_count = lax.axis_size("row")
    row_index = lax.axis_index("row")
    flat_index = lax.axis_index("ctx") * row_count + row_index
    own_query = queries.reshape(rows_dev, step_count, KVH, groups, HD)
    slot_count, page_len, kv_width = pool_keys.shape
    slot_ids = flat_index * slot_count + jnp.arange(slot_count, dtype=jnp.int32)
    slot_match = page_table[:, :, None] == slot_ids[None, None, :]
    entry_pos = jnp.arange(page_table.shape[1], dtype=jnp.int32)
    page_of = jnp.sum(jnp.where(slot_match, entry_pos[None, :, None], 0), axis=1)
    owned = jnp.any(slot_match, axis=1)
    token_pos = (
        page_of[:, :, None] * page_len + jnp.arange(page_len, dtype=jnp.int32)[None, None, :]
    )
    live_mask = owned[:, :, None] & (token_pos < suffix_len[:, None, None])
    live_mask = live_mask.reshape(rows_dev, 1, 1, 1, slot_count * page_len)
    flat_keys = pool_keys.reshape(slot_count * page_len, KVH, HD)
    flat_values = pool_values.reshape(slot_count * page_len, KVH, HD)
    suffix_scores = (
        jnp.einsum("rskgd,tkd->rskgt", own_query, flat_keys, preferred_element_type=jnp.float32)
        * score_scale
    )
    suffix_stats = block_stats(suffix_scores, live_mask, flat_values, "rskgt,tkd->rskgd")
    fresh_keys = new_keys.reshape(rows_dev, step_count, KVH, HD)
    fresh_values = new_values.reshape(rows_dev, step_count, KVH, HD)
    fresh_scores = (
        jnp.einsum("rskgd,rtkd->rskgt", own_query, fresh_keys, preferred_element_type=jnp.float32)
        * score_scale
    )
    causal = jnp.arange(step_count)[None, :] <= jnp.arange(step_count)[:, None]
    causal = causal.reshape(1, step_count, 1, 1, step_count)
    fresh_stats = heads_merged(block_stats(fresh_scores, causal, fresh_values, "rskgt,rtkd->rskgd"))
    every_query, every_prefix = (
        lax.all_gather(queries, "row", axis=0, tiled=True),
        lax.all_gather(prefix_id, "row", axis=0, tiled=True),
    )
    total_rows = every_query.shape[0]
    span_len = prefix_keys.shape[1]
    row_keys = jnp.take(prefix_keys, every_prefix, axis=0).reshape(total_rows, span_len, KVH, HD)
    row_values = jnp.take(prefix_values, every_prefix, axis=0).reshape(
        total_rows, span_len, KVH, HD
    )
    every_row = every_query.reshape(total_rows, step_count, KVH, groups, HD)
    prefix_scores = (
        jnp.einsum("rskgd,rtkd->rskgt", every_row, row_keys, preferred_element_type=jnp.float32)
        * score_scale
    )
    always = jnp.ones((1, 1, 1, 1, span_len), dtype=bool)
    prefix_stats = block_stats(prefix_scores, always, row_values, "rskgt,rtkd->rskgd")
    row_start = row_index * rows_dev
    own_prefix = tuple(
        (lax.dynamic_slice_in_dim(member, row_start, rows_dev, 0) for member in prefix_stats)
    )
    own_merged = combine_pair(own_prefix, suffix_stats)
    whole_stats = tuple(
        (
            lax.dynamic_update_slice_in_dim(whole_arr, piece_arr, row_start, 0)
            for whole_arr, piece_arr in zip(prefix_stats, own_merged)
        )
    )
    block_peak, block_total, block_sum = heads_merged(whole_stats)
    stacked = (
        lax.all_to_all(block_peak[None], "row", split_axis=1, concat_axis=0, tiled=True),
        lax.all_to_all(block_total[None], "row", split_axis=1, concat_axis=0, tiled=True),
        lax.all_to_all(block_sum[None], "row", split_axis=1, concat_axis=0, tiled=True),
    )
    local_stats = fold_stack(stacked)
    merged = joined(local_stats, "ctx", combine_pair)
    final_stats = combine_pair(merged, fresh_stats)
    result = (final_stats[2] / final_stats[1][..., None]).astype(jnp.bfloat16)
    return result.reshape(rows_dev, step_count, H * HD)


def solution(mesh):
    in_specs = (
        P("row", None, None),
        P("row"),
        P(None, ("ctx", "row"), None),
        P(None, ("ctx", "row"), None),
        P(("ctx", "row"), None, None),
        P(("ctx", "row"), None, None),
        P("row", None),
        P("row"),
        P("row", None, None),
        P("row", None, None),
    )
    out_specs = P("row", None, None)
    return jax.shard_map(
        per_device, mesh=mesh, in_specs=in_specs, out_specs=out_specs, check_vma=False
    )
```

profile of v0, /device:TPU:0, one launch (start us, length us, event | category | flops | bytes accessed | tf_op | source)
XLA Modules:
  0.0 102.8 jit_solution(12264209918332326410)
XLA Ops:
  0.0 0.9 compare_reduce_fusion
  0.9 0.9 fusion.21
  1.8 0.6 copy-done.11
  3.7 0.6 copy-done.10
  4.5 13.1 %all-reduce = s32[16]{0:T(128)S(1)} all-reduce(s32[16]{0:T(128)S(1)} %dynamic-update-slice), channel_id=1, replica_groups=mesh['ctx'=4,'row'=8] {'row'}, use_global_device_ids=true, to_apply=%add | all-reduce | flops 16 | bytes 128
  17.6 30.8 %all_gather.25 = bf16[16,2,4096]{2,1,0:T(2,128)(2,1)S(1)} all-gather(bf16[2,2,4096]{2,1,0:T(2,128)(2,1)S(1)} %copy-done.4), channel_id=1, replica_groups=mesh['ctx'=4,'row'=8] {'row'}, dimensions={0}, use_global_device_ids=true | all-gather | bytes 294912 | tf_op jit(solution)/shard_map/all_gather | solution.py:107
  52.3 0.9 copy-done.1
  53.5 0.6 copy-done.8
  54.8 0.9 convert_reduce_fusion
  55.8 0.7 reshape.185
  56.5 3.3 %all-to-all-start.1 = ((f32[8,1,128]{2,1,0:T(1,128)}), f32[8,1,128]{2,1,0:T(1,128)S(1)}, u32[]{:S(2)}, u32[]{:S(2)}) async-start(f32[8,1,128]{2,1,0:T(1,128)} %reshape.185), calls=%async_computation.1 | async-start | bytes 8192 | tf_op jit(solution)/shard_map/all_to_all | solution.py:137
  60.1 0.7 reshape.183
  61.1 5.2 %all-to-all-done.1 = f32[8,1,128]{2,1,0:T(1,128)S(1)} async-done(((f32[8,1,128]{2,1,0:T(1,128)}), f32[8,1,128]{2,1,0:T(1,128)S(1)}, u32[]{:S(2)}, u32[]{:S(2)}) %all-to-all-start.1) | async-done | bytes 4128 | tf_op jit(solution)/shard_map/all_to_all | solution.py:137
  66.3 3.3 %all-to-all-start = ((f32[8,1,128]{2,1,0:T(1,128)}), f32[8,1,128]{2,1,0:T(1,128)S(1)}, u32[]{:S(2)}, u32[]{:S(2)}) async-start(f32[8,1,128]{2,1,0:T(1,128)} %reshape.183), calls=%async_computation | async-start | bytes 8192 | tf_op jit(solution)/shard_map/all_to_all | solution.py:136
  69.6 1.2 %fusion.7 = f32[16,2,4,8,128]{4,3,1,2,0:T(8,128)S(1)} fusion(f32[16,2,4,8,128]{4,3,1,2,0:T(8,128)S(1)} %copy.183, s32[]{:T(128)S(6)} %select_n.36, bf16[1024,4,128,1,1]{2,1,0,4,3:T(4,128)(2,1)S(1)} %bitcast.92, bf16[2,2,4,8,1024]{4,3,1,0,2:T(8,128)(2,1)} %get-tuple-element.77, f32[16,4,128,2,8]{2,4,3,1,0:T(8,128)S(1)} %fusion.11, ...), kind=kOutput, calls=%fused_computation.18 | convolution fusion | flops 33603584 | bytes 1458180 | tf_op jit(solution)/shard_map/rskgt,tkd->rskgd/dot_general | solution.py:47
  70.8 0.9 copy.179
  71.7 4.4 %all-to-all-done = f32[8,1,128]{2,1,0:T(1,128)S(1)} async-done(((f32[8,1,128]{2,1,0:T(1,128)}), f32[8,1,128]{2,1,0:T(1,128)S(1)}, u32[]{:S(2)}, u32[]{:S(2)}) %all-to-all-start) | async-done | bytes 4128 | tf_op jit(solution)/shard_map/all_to_all | solution.py:136
  76.1 3.6 %all-to-all-start.2 = ((f32[1,16,2,32,128]{4,3,2,0,1:T(8,128)}), f32[1,16,2,32,128]{4,3,2,0,1:T(8,128)S(1)}, u32[]{:S(2)}, u32[]{:S(2)}) async-start(f32[1,16,2,32,128]{4,3,2,0,1:T(8,128)} %bitcast.84), calls=%async_computation.2 | async-start | bytes 1048576 | tf_op jit(solution)/shard_map/all_to_all | solution.py:138
  81.6 0.7 reduce.1
  82.4 0.7 reduce
  83.2 5.2 %all-gather.1 = f32[8,2,32]{2,1,0:T(2,128)S(1)} all-gather(f32[2,2,32]{2,1,0:T(2,128)S(1)} %copy.107), channel_id=3, replica_groups=mesh['ctx'=4,'row'=8] {'ctx'}, dimensions={0}, use_global_device_ids=true | all-gather | bytes 2560 | tf_op jit(solution)/shard_map/all_gather | solution.py:14
  89.0 5.1 %all-gather = f32[8,2,32]{2,1,0:T(2,128)S(1)} all-gather(f32[2,2,32]{2,1,0:T(2,128)S(1)} %copy.101), channel_id=2, replica_groups=mesh['ctx'=4,'row'=8] {'ctx'}, dimensions={0}, use_global_device_ids=true | all-gather | bytes 2560 | tf_op jit(solution)/shard_map/all_gather | solution.py:14
  95.0 5.8 %all-gather.2 = f32[8,2,32,128]{3,2,1,0:T(8,128)S(1)} all-gather(f32[2,2,32,128]{3,2,1,0:T(8,128)S(1)} %multiply_reduce_fusion), channel_id=4, replica_groups=mesh['ctx'=4,'row'=8] {'ctx'}, dimensions={0}, use_global_device_ids=true | all-gather | bytes 327680 | tf_op jit(solution)/shard_map/all_gather | solution.py:14
  100.8 0.7 slice-done
  (91 shorter events, 11.4 us)
Async XLA Ops:
  0.0 49.0 %copy-start = (bf16[8,32,512]{2,1,0:T(8,128)(2,1)S(1)}, bf16[8,32,512]{2,1,0:T(8,128)(2,1)}, u32[]{:S(2)}) copy-start(bf16[8,32,512]{2,1,0:T(8,128)(2,1)} %param.17) | copy-start | bytes 786436
  0.0 17.6 %copy-start.4 = (bf16[2,2,4096]{2,1,0:T(2,128)(2,1)S(1)}, bf16[2,2,4096]{2,1,0:T(2,128)(2,1)}, u32[]{:S(2)}) copy-start(bf16[2,2,4096]{2,1,0:T(2,128)(2,1)} %param.14) | copy-start | bytes 98308
  1.8 0.7 copy-start.11
  3.7 0.7 copy-start.10
  49.1 1.0 copy-start.3
  52.0 1.2 %copy-start.1 = (bf16[16,64,512]{2,1,0:T(8,128)(2,1)S(1)}, bf16[16,64,512]{2,1,0:T(8,128)(2,1)}, u32[]{:S(2)}) copy-start(bf16[16,64,512]{2,1,0:T(8,128)(2,1)} %param.18) | copy-start | bytes 3145732
  53.5 0.7 copy-start.8
  54.8 6.0 %copy-start.2 = (bf16[16,64,512]{2,1,0:T(8,128)(2,1)S(1)}, bf16[16,64,512]{2,1,0:T(8,128)(2,1)}, u32[]{:S(2)}) copy-start(bf16[16,64,512]{2,1,0:T(8,128)(2,1)} %param.19) | copy-start | bytes 3145732
  56.5 9.7 %all-to-all-start.1 = ((f32[8,1,128]{2,1,0:T(1,128)}), f32[8,1,128]{2,1,0:T(1,128)S(1)}, u32[]{:S(2)}, u32[]{:S(2)}) async-start(f32[8,1,128]{2,1,0:T(1,128)} %reshape.185), calls=%async_computation.1 | async-start | bytes 8192 | tf_op jit(solution)/shard_map/all_to_all | solution.py:137
  66.3 9.8 %all-to-all-start = ((f32[8,1,128]{2,1,0:T(1,128)}), f32[8,1,128]{2,1,0:T(1,128)S(1)}, u32[]{:S(2)}, u32[]{:S(2)}) async-start(f32[8,1,128]{2,1,0:T(1,128)} %reshape.183), calls=%async_computation | async-start | bytes 8192 | tf_op jit(solution)/shard_map/all_to_all | solution.py:136
  76.1 3.6 %copy-start.9 = (bf16[2,2,512]{2,1,0:T(2,128)(2,1)S(1)}, bf16[2,2,512]{2,1,0:T(2,128)(2,1)}, u32[]{:S(2)}) copy-start(bf16[2,2,512]{2,1,0:T(2,128)(2,1)} %param.22) | copy-start | bytes 12292
  76.1 18.7 %all-to-all-start.2 = ((f32[1,16,2,32,128]{4,3,2,0,1:T(8,128)}), f32[1,16,2,32,128]{4,3,2,0,1:T(8,128)S(1)}, u32[]{:S(2)}, u32[]{:S(2)}) async-start(f32[1,16,2,32,128]{4,3,2,0,1:T(8,128)} %bitcast.84), calls=%async_computation.2 | async-start | bytes 1048576 | tf_op jit(solution)/shard_map/all_to_all | solution.py:138
  80.2 0.7 copy-start.7
  88.4 0.6 copy-start.5
  94.1 0.6 copy-start.6
  100.8 0.7 slice-start
  100.8 0.7 slice-start.1
where the time goes:
time: 103 us
  blocking collectives  60 us (58%)
  local copies, waits for them, and re-layouts  13.1 us (13%)
  starting transfers between devices  10.3 us (10%)
  waiting for transfers between devices  9.62 us (9%)
  other arithmetic  5.62 us (5%)
  matrix products  3.1 us (3%)
    all_gather x1, blocking collectives, per_device(): lax.all_gather(queries, 'row', axis=0, tiled=True)  30.8 us
    all_gather x3, blocking collectives, joined(): pieces = jax.tree.map(lambda part: lax.all_gather(part, axis), value)  16.1 us
    unnamed x1, blocking collectives  13.1 us
    unnamed x32, local copies, waits for them, and re-layouts  7.34 us
    all_to_all x1, waiting for transfers between devices, per_device(): lax.all_to_all(block_total[None], 'row', split_axis=1, concat_axis=0, til...  5.21 us
    all_to_all x1, waiting for transfers between devices, per_device(): lax.all_to_all(block_peak[None], 'row', split_axis=1, concat_axis=0, tile...  4.41 us
    all_to_all x1, starting transfers between devices, per_device(): lax.all_to_all(block_sum[None], 'row', split_axis=1, concat_axis=0, tiled...  3.62 us
    all_to_all x1, starting transfers between devices, per_device(): lax.all_to_all(block_total[None], 'row', split_axis=1, concat_axis=0, til...  3.32 us
  transfers between devices with their start and end apart: 3, of which 2 were waited for; matrix products, arithmetic and copies ran while one was open for 6% of the time, Pallas kernels for 0%

commit v1 on v0

--- a/solution.py
+++ b/solution.py
@@ -8,6 +8,27 @@
 KVH = 4
 HD = 128
 MASKED_SCORE = -1e30
+
+
+def gather_around(array, axis, dim):
+    size, here, span = (lax.axis_size(axis), lax.axis_index(axis), array.shape[dim])
+    right = [(i, (i + 1) % size) for i in range(size)]
+    left = [(i, (i - 1) % size) for i in range(size)]
+    whole = jnp.zeros((*array.shape[:dim], size * span, *array.shape[dim + 1 :]), array.dtype)
+    whole = lax.dynamic_update_slice_in_dim(whole, array, here * span, axis=dim)
+    from_left = from_right = array
+    halfway = size // 2
+    for step in range(1, halfway + 1):
+        from_left = lax.ppermute(from_left, axis, right)
+        whole = lax.dynamic_update_slice_in_dim(
+            whole, from_left, (here - step) % size * span, axis=dim
+        )
+        if step < size - halfway:
+            from_right = lax.ppermute(from_right, axis, left)
+            whole = lax.dynamic_update_slice_in_dim(
+                whole, from_right, (here + step) % size * span, axis=dim
+            )
+    return whole
 
 
 def joined(value, axis, join):
@@ -104,7 +125,7 @@
     causal = causal.reshape(1, step_count, 1, 1, step_count)
     fresh_stats = heads_merged(block_stats(fresh_scores, causal, fresh_values, "rskgt,rtkd->rskgd"))
     every_query, every_prefix = (
-        lax.all_gather(queries, "row", axis=0, tiled=True),
+        gather_around(queries, "row", 0),
         lax.all_gather(prefix_id, "row", axis=0, tiled=True),
     )
     total_rows = every_query.shape[0]

time: 103 us -> 97.1 us (0.943)
  blocking collectives: 60 us -> 26.1 us
  starting transfers between devices: 10.3 us -> 25.8 us
  waiting for transfers between devices: 9.62 us -> 17.1 us
  local copies, waits for them, and re-layouts: 13.1 us -> 18.8 us
    all_gather x1 -> x0, blocking collectives: 30.8 us -> none  [per_device(): lax.all_gather(queries, 'row', axis=0, tiled=True)]
    ppermute x0 -> x7, starting transfers between devices: none -> 15.5 us  [the longest x3 12 us: gather_around(): from_right = lax.ppermute(from_right, axis, left)]
    ppermute x0 -> x7, waiting for transfers between devices: none -> 6.57 us  [the longest x4 6.57 us: gather_around(): from_left = lax.ppermute(from_left, axis, right)]
    dynamic_update_slice x0 -> x8, local copies, waits for them, and re-layouts: none -> 5.2 us  [the longest x4 2.57 us: gather_around(): lax.dynamic_update_slice_in_dim(whole, from_left, (here - step) % size *...]
    unnamed x1, blocking collectives: 13.1 us -> 9.94 us
    unnamed x32 -> x35, local copies, waits for them, and re-layouts: 7.34 us -> 7.21 us
  transfers between devices with their start and end apart: 3 -> 10, of which waited for: 2 -> 5; matrix products, arithmetic and copies ran while one was open for 6% -> 17% of each run, Pallas kernels for 0% -> 0%
where the time goes in v1:
time: 97.1 us; the launch traced here: 96.5 us
  blocking collectives  26.1 us (27%)
  starting transfers between devices  25.8 us (27%)
  local copies, waits for them, and re-layouts  18.8 us (19%)
  waiting for transfers between devices  17.1 us (18%)
  other arithmetic  5.46 us (6%)
  matrix products  2.15 us (2%)
  between operations  1.18 us (1%)
    all_gather x3, blocking collectives, joined(): pieces = jax.tree.map(lambda part: lax.all_gather(part, axis), value)  16.1 us
    ppermute x3, starting transfers between devices, gather_around(): from_right = lax.ppermute(from_right, axis, left)  12 us
    unnamed x1, blocking collectives  9.94 us
    unnamed x35, local copies, waits for them, and re-layouts  7.21 us
    ppermute x4, waiting for transfers between devices, gather_around(): from_left = lax.ppermute(from_left, axis, right)  6.57 us
    all_to_all x1, waiting for transfers between devices, per_device(): lax.all_to_all(block_peak[None], 'row', split_axis=1, concat_axis=0, tile...  5.29 us
    all_to_all x1, waiting for transfers between devices, per_device(): lax.all_to_all(block_total[None], 'row', split_axis=1, concat_axis=0, til...  5.19 us
    all_to_all x1, starting transfers between devices, per_device(): lax.all_to_all(block_sum[None], 'row', split_axis=1, concat_axis=0, tiled...  3.62 us
  transfers between devices with their start and end apart: 10, of which 5 were waited for; matrix products, arithmetic and copies ran while one was open for 17% of the time, Pallas kernels for 0%

profile of v1, /device:TPU:0, one launch (start us, length us, event | category | flops | bytes accessed | tf_op | source)
XLA Modules:
  0.0 96.5 jit_solution(8057482039200172058)
XLA Ops:
  0.0 2.9 %collective-permute-start = (bf16[2,2,4096]{2,1,0:T(2,128)(2,1)}, bf16[2,2,4096]{2,1,0:T(2,128)(2,1)S(1)}, u32[]{:S(2)}, u32[]{:S(2)}) collective-permute-start(bf16[2,2,4096]{2,1,0:T(2,128)(2,1)} %param.14), channel_id=1, source_target_pairs={{0,1},{1,2},{2,3},{3,4},{4,5},{5,6},{6,7},{7,0},{8,9},{9,10},{10,1... | collective-permute-start | bytes 98312 | tf_op jit(solution)/shard_map/ppermute | solution.py:22
  2.9 3.1 %collective-permute-start.1 = (bf16[2,2,4096]{2,1,0:T(2,128)(2,1)}, bf16[2,2,4096]{2,1,0:T(2,128)(2,1)S(1)}, u32[]{:S(2)}, u32[]{:S(2)}) collective-permute-start(bf16[2,2,4096]{2,1,0:T(2,128)(2,1)} %param.14), channel_id=1, source_target_pairs={{0,7},{1,0},{2,1},{3,2},{4,3},{5,4},{6,5},{7,6},{8,15},{9,8},{10,9... | collective-permute-start | bytes 98312 | tf_op jit(solution)/shard_map/ppermute | solution.py:27
  6.0 0.9 compare_reduce_fusion
  6.9 0.9 fusion.21
  10.5 9.9 %all-reduce = s32[16]{0:T(128)S(1)} all-reduce(s32[16]{0:T(128)S(1)} %dynamic-update-slice), channel_id=1, replica_groups=mesh['ctx'=4,'row'=8] {'row'}, use_global_device_ids=true, to_apply=%add | all-reduce | flops 16 | bytes 128
  23.2 0.7 broadcast_in_dim.96
  23.9 0.7 copy_dynamic-update-slice_fusion.7
  27.2 4.1 %collective-permute-start.3 = (bf16[2,2,4096]{2,1,0:T(2,128)(2,1)S(1)}, bf16[2,2,4096]{2,1,0:T(2,128)(2,1)S(1)}, u32[]{:S(2)}, u32[]{:S(2)}) collective-permute-start(bf16[2,2,4096]{2,1,0:T(2,128)(2,1)S(1)} %collective-permute-done.1), channel_id=1, source_target_pairs={{0,7},{1,0},{2,1},{3,2},{4,3},{5,4},{6,5},{7,6},{8,15},{9,8},{10,9... | collective-permute-start | bytes 98312 | tf_op jit(solution)/shard_map/ppermute | solution.py:27
  33.2 4.7 %collective-permute-start.5 = (bf16[2,2,4096]{2,1,0:T(2,128)(2,1)S(1)}, bf16[2,2,4096]{2,1,0:T(2,128)(2,1)S(1)}, u32[]{:S(2)}, u32[]{:S(2)}) collective-permute-start(bf16[2,2,4096]{2,1,0:T(2,128)(2,1)S(1)} %collective-permute-done.3), channel_id=1, source_target_pairs={{0,7},{1,0},{2,1},{3,2},{4,3},{5,4},{6,5},{7,6},{8,15},{9,8},{10,9... | collective-permute-start | bytes 98312 | tf_op jit(solution)/shard_map/ppermute | solution.py:27
  39.2 0.7 collective-permute-done.4
  40.6 0.7 copy_dynamic-update-slice_fusion.1
  41.2 5.3 %collective-permute-done.6 = bf16[2,2,4096]{2,1,0:T(2,128)(2,1)S(1)} collective-permute-done((bf16[2,2,4096]{2,1,0:T(2,128)(2,1)S(1)}, bf16[2,2,4096]{2,1,0:T(2,128)(2,1)S(1)}, u32[]{:S(2)}, u32[]{:S(2)}) %collective-permute-start.6) | collective-permute-done | bytes 32800 | tf_op jit(solution)/shard_map/ppermute | solution.py:22
  47.2 1.0 %copy.162 = bf16[4,8,32,128]{3,2,1,0:T(8,128)(2,1)S(1)} copy(bf16[4,8,32,128]{3,1,2,0:T(8,128)(2,1)} %bitcast.39) | data formatting | bytes 524288
  49.7 0.7 reshape.184
  50.4 3.3 %all-to-all-start.1 = ((f32[8,1,128]{2,1,0:T(1,128)}), f32[8,1,128]{2,1,0:T(1,128)S(1)}, u32[]{:S(2)}, u32[]{:S(2)}) async-start(f32[8,1,128]{2,1,0:T(1,128)} %reshape.184), calls=%async_computation.1 | async-start | bytes 8192 | tf_op jit(solution)/shard_map/all_to_all | solution.py:158
  54.2 0.7 reshape.182
  54.9 5.2 %all-to-all-done.1 = f32[8,1,128]{2,1,0:T(1,128)S(1)} async-done(((f32[8,1,128]{2,1,0:T(1,128)}), f32[8,1,128]{2,1,0:T(1,128)S(1)}, u32[]{:S(2)}, u32[]{:S(2)}) %all-to-all-start.1) | async-done | bytes 4128 | tf_op jit(solution)/shard_map/all_to_all | solution.py:158
  60.1 3.3 %all-to-all-start = ((f32[8,1,128]{2,1,0:T(1,128)}), f32[8,1,128]{2,1,0:T(1,128)S(1)}, u32[]{:S(2)}, u32[]{:S(2)}) async-start(f32[8,1,128]{2,1,0:T(1,128)} %reshape.182), calls=%async_computation | async-start | bytes 8192 | tf_op jit(solution)/shard_map/all_to_all | solution.py:157
  63.7 0.9 copy.214
  64.6 5.3 %all-to-all-done = f32[8,1,128]{2,1,0:T(1,128)S(1)} async-done(((f32[8,1,128]{2,1,0:T(1,128)}), f32[8,1,128]{2,1,0:T(1,128)S(1)}, u32[]{:S(2)}, u32[]{:S(2)}) %all-to-all-start) | async-done | bytes 4128 | tf_op jit(solution)/shard_map/all_to_all | solution.py:157
  69.9 3.6 %all-to-all-start.2 = ((f32[1,16,2,32,128]{4,3,2,0,1:T(8,128)}), f32[1,16,2,32,128]{4,3,2,0,1:T(8,128)S(1)}, u32[]{:S(2)}, u32[]{:S(2)}) async-start(f32[1,16,2,32,128]{4,3,2,0,1:T(8,128)} %bitcast.90), calls=%async_computation.2 | async-start | bytes 1048576 | tf_op jit(solution)/shard_map/all_to_all | solution.py:159
  77.0 5.2 %all-gather.1 = f32[8,2,32]{2,1,0:T(2,128)S(1)} all-gather(f32[2,2,32]{2,1,0:T(2,128)S(1)} %copy.135), channel_id=3, replica_groups=mesh['ctx'=4,'row'=8] {'ctx'}, dimensions={0}, use_global_device_ids=true | all-gather | bytes 2560 | tf_op jit(solution)/shard_map/all_gather | solution.py:35
  82.8 5.1 %all-gather = f32[8,2,32]{2,1,0:T(2,128)S(1)} all-gather(f32[2,2,32]{2,1,0:T(2,128)S(1)} %copy.129), channel_id=2, replica_groups=mesh['ctx'=4,'row'=8] {'ctx'}, dimensions={0}, use_global_device_ids=true | all-gather | bytes 2560 | tf_op jit(solution)/shard_map/all_gather | solution.py:35
  88.7 5.8 %all-gather.2 = f32[8,2,32,128]{3,2,1,0:T(8,128)S(1)} all-gather(f32[2,2,32,128]{3,2,1,0:T(8,128)S(1)} %multiply_reduce_fusion), channel_id=4, replica_groups=mesh['ctx'=4,'row'=8] {'ctx'}, dimensions={0}, use_global_device_ids=true | all-gather | bytes 327680 | tf_op jit(solution)/shard_map/all_gather | solution.py:35
  (115 shorter events, 21.1 us)
Async XLA Ops:
  0.0 21.4 %copy-start = (bf16[8,32,512]{2,1,0:T(8,128)(2,1)S(1)}, bf16[8,32,512]{2,1,0:T(8,128)(2,1)}, u32[]{:S(2)}) copy-start(bf16[8,32,512]{2,1,0:T(8,128)(2,1)} %param.17) | copy-start | bytes 786436
  0.0 21.0 %copy-start.4 = (bf16[2,2,4096]{2,1,0:T(2,128)(2,1)S(1)}, bf16[2,2,4096]{2,1,0:T(2,128)(2,1)}, u32[]{:S(2)}) copy-start(bf16[2,2,4096]{2,1,0:T(2,128)(2,1)} %param.14) | copy-start | bytes 98308
  0.0 26.5 %collective-permute-start = (bf16[2,2,4096]{2,1,0:T(2,128)(2,1)}, bf16[2,2,4096]{2,1,0:T(2,128)(2,1)S(1)}, u32[]{:S(2)}, u32[]{:S(2)}) collective-permute-start(bf16[2,2,4096]{2,1,0:T(2,128)(2,1)} %param.14), channel_id=1, source_target_pairs={{0,1},{1,2},{2,3},{3,4},{4,5},{5,6},{6,7},{7,0},{8,9},{9,10},{10,1... | collective-permute-start | bytes 98312 | tf_op jit(solution)/shard_map/ppermute | solution.py:22
  2.9 24.2 %collective-permute-start.1 = (bf16[2,2,4096]{2,1,0:T(2,128)(2,1)}, bf16[2,2,4096]{2,1,0:T(2,128)(2,1)S(1)}, u32[]{:S(2)}, u32[]{:S(2)}) collective-permute-start(bf16[2,2,4096]{2,1,0:T(2,128)(2,1)} %param.14), channel_id=1, source_target_pairs={{0,7},{1,0},{2,1},{3,2},{4,3},{5,4},{6,5},{7,6},{8,15},{9,8},{10,9... | collective-permute-start | bytes 98312 | tf_op jit(solution)/shard_map/ppermute | solution.py:27
  7.8 0.7 copy-start.12
  9.7 0.7 copy-start.11
  21.3 1.0 copy-start.3
  21.4 1.5 %copy-start.1 = (bf16[16,64,512]{2,1,0:T(8,128)(2,1)S(1)}, bf16[16,64,512]{2,1,0:T(8,128)(2,1)}, u32[]{:S(2)}) copy-start(bf16[16,64,512]{2,1,0:T(8,128)(2,1)} %param.18) | copy-start | bytes 3145732
  23.9 0.7 copy-start.8
  24.6 0.7 copy-start.9
  26.5 6.7 %collective-permute-start.2 = (bf16[2,2,4096]{2,1,0:T(2,128)(2,1)S(1)}, bf16[2,2,4096]{2,1,0:T(2,128)(2,1)S(1)}, u32[]{:S(2)}, u32[]{:S(2)}) collective-permute-start(bf16[2,2,4096]{2,1,0:T(2,128)(2,1)S(1)} %collective-permute-done), channel_id=1, source_target_pairs={{0,1},{1,2},{2,3},{3,4},{4,5},{5,6},{6,7},{7,0},{8,9},{9,10},{10,1... | collective-permute-start | bytes 98312 | tf_op jit(solution)/shard_map/ppermute | solution.py:22
  27.2 6.0 %collective-permute-start.3 = (bf16[2,2,4096]{2,1,0:T(2,128)(2,1)S(1)}, bf16[2,2,4096]{2,1,0:T(2,128)(2,1)S(1)}, u32[]{:S(2)}, u32[]{:S(2)}) collective-permute-start(bf16[2,2,4096]{2,1,0:T(2,128)(2,1)S(1)} %collective-permute-done.1), channel_id=1, source_target_pairs={{0,7},{1,0},{2,1},{3,2},{4,3},{5,4},{6,5},{7,6},{8,15},{9,8},{10,9... | collective-permute-start | bytes 98312 | tf_op jit(solution)/shard_map/ppermute | solution.py:27
  33.2 6.7 %collective-permute-start.4 = (bf16[2,2,4096]{2,1,0:T(2,128)(2,1)S(1)}, bf16[2,2,4096]{2,1,0:T(2,128)(2,1)S(1)}, u32[]{:S(2)}, u32[]{:S(2)}) collective-permute-start(bf16[2,2,4096]{2,1,0:T(2,128)(2,1)S(1)} %collective-permute-done.2), channel_id=1, source_target_pairs={{0,1},{1,2},{2,3},{3,4},{4,5},{5,6},{6,7},{7,0},{8,9},{9,10},{10,1... | collective-permute-start | bytes 98312 | tf_op jit(solution)/shard_map/ppermute | solution.py:22
  33.2 7.4 %collective-permute-start.5 = (bf16[2,2,4096]{2,1,0:T(2,128)(2,1)S(1)}, bf16[2,2,4096]{2,1,0:T(2,128)(2,1)S(1)}, u32[]{:S(2)}, u32[]{:S(2)}) collective-permute-start(bf16[2,2,4096]{2,1,0:T(2,128)(2,1)S(1)} %collective-permute-done.3), channel_id=1, source_target_pairs={{0,7},{1,0},{2,1},{3,2},{4,3},{5,4},{6,5},{7,6},{8,15},{9,8},{10,9... | collective-permute-start | bytes 98312 | tf_op jit(solution)/shard_map/ppermute | solution.py:27
  39.9 6.6 %collective-permute-start.6 = (bf16[2,2,4096]{2,1,0:T(2,128)(2,1)S(1)}, bf16[2,2,4096]{2,1,0:T(2,128)(2,1)S(1)}, u32[]{:S(2)}, u32[]{:S(2)}) collective-permute-start(bf16[2,2,4096]{2,1,0:T(2,128)(2,1)S(1)} %collective-permute-done.4), channel_id=1, source_target_pairs={{0,1},{1,2},{2,3},{3,4},{4,5},{5,6},{6,7},{7,0},{8,9},{9,10},{10,1... | collective-permute-start | bytes 98312 | tf_op jit(solution)/shard_map/ppermute | solution.py:22
  49.1 4.6 %copy-start.2 = (bf16[16,64,512]{2,1,0:T(8,128)(2,1)S(1)}, bf16[16,64,512]{2,1,0:T(8,128)(2,1)}, u32[]{:S(2)}) copy-start(bf16[16,64,512]{2,1,0:T(8,128)(2,1)} %param.19) | copy-start | bytes 3145732
  50.4 9.7 %all-to-all-start.1 = ((f32[8,1,128]{2,1,0:T(1,128)}), f32[8,1,128]{2,1,0:T(1,128)S(1)}, u32[]{:S(2)}, u32[]{:S(2)}) async-start(f32[8,1,128]{2,1,0:T(1,128)} %reshape.184), calls=%async_computation.1 | async-start | bytes 8192 | tf_op jit(solution)/shard_map/all_to_all | solution.py:158
  60.1 9.8 %all-to-all-start = ((f32[8,1,128]{2,1,0:T(1,128)}), f32[8,1,128]{2,1,0:T(1,128)S(1)}, u32[]{:S(2)}, u32[]{:S(2)}) async-start(f32[8,1,128]{2,1,0:T(1,128)} %reshape.182), calls=%async_computation | async-start | bytes 8192 | tf_op jit(solution)/shard_map/all_to_all | solution.py:157
  69.9 3.6 %copy-start.10 = (bf16[2,2,512]{2,1,0:T(2,128)(2,1)S(1)}, bf16[2,2,512]{2,1,0:T(2,128)(2,1)}, u32[]{:S(2)}) copy-start(bf16[2,2,512]{2,1,0:T(2,128)(2,1)} %param.22) | copy-start | bytes 12292
  69.9 18.7 %all-to-all-start.2 = ((f32[1,16,2,32,128]{4,3,2,0,1:T(8,128)}), f32[1,16,2,32,128]{4,3,2,0,1:T(8,128)S(1)}, u32[]{:S(2)}, u32[]{:S(2)}) async-start(f32[1,16,2,32,128]{4,3,2,0,1:T(8,128)} %bitcast.90), calls=%async_computation.2 | async-start | bytes 1048576 | tf_op jit(solution)/shard_map/all_to_all | solution.py:159
  74.0 0.7 copy-start.7
  87.9 0.6 copy-start.6
  94.6 0.7 slice-start
  94.6 0.7 slice-start.1
  (1 other events, 0.6 us)
